TPU v7x, 256 devices: a whole 4x4x8 slice. The times are simulated.
256 devices in a mesh: req: 32 (over z, x), head: 4 (over y), blk: 2 (over core).
Axes of the slice: x: 4, y: 4, z: 8, core: 2. Of those that a mesh axis runs over, the one named last changes fastest.
Arguments:
- x_tokens: bfloat16 [32, 512, 1024], P('req', ('head', 'blk')), may hold values from -40 to 40
- query: bfloat16 [32, 512, 1024], P('req', None, ('head', 'blk')), may hold values from -200 to 200
- key_new: bfloat16 [32, 512, 1024], P('req', None, ('head', 'blk')), may hold values from -4 to 4
- value_new: bfloat16 [32, 512, 1024], P('req', None, ('head', 'blk')), may hold values from -4 to 4
- cache_keys: bfloat16 [32, 2048, 1024], P('req', None, ('head', 'blk')), may hold values from -4 to 4
- cache_values: bfloat16 [32, 2048, 1024], P('req', None, ('head', 'blk')), may hold values from -4 to 4
- prefix_keys: bfloat16 [4, 512, 1024], P(None, None, ('head', 'blk')), may hold values from -4 to 4
- prefix_values: bfloat16 [4, 512, 1024], P(None, None, ('head', 'blk')), may hold values from -4 to 4
- history_len: int32 [32], P('req'), may hold values from 512 to 2048, as said below
- group_ids: int32 [32], P('req'), may hold values from 0 to 3
- out_weight: bfloat16 [1024, 1024], P(('head', 'blk')), may hold values from -0.1875 to 0.1875
- norm_gain: float32 [1024], replicated, may hold values from 0.5 to 1.5
- router_weight: bfloat16 [1024, 16], replicated, may hold values from -0.1875 to 0.1875
- expert_gate: bfloat16 [1024, 45056], P(None, ('req', 'head')), may hold values from -0.1875 to 0.1875
- expert_up: bfloat16 [1024, 45056], P(None, ('req', 'head')), may hold values from -0.1875 to 0.1875
- expert_down: bfloat16 [45056, 1024], P(('req', 'head')), may hold values from -0.109375 to 0.109375
- expert_ids: int32 [32, 512, 2], P('req', ('head', 'blk')), may hold values from 0 to 15, all different within a row; in each aligned block of 64 rows (0 to 63, 64 to 127, ..., all dimensions but the last counted through in order) at most 16 rows name the same one
- keep_mask: int32 [32, 512, 2], P('req', ('head', 'blk')), may hold values 0 or 1
Outputs:
- y_out: bfloat16 [32, 512, 1024], P('req', ('head', 'blk'))
- new_keys: bfloat16 [32, 2560, 1024], P('req', ('head', 'blk'))
- new_values: bfloat16 [32, 2560, 1024], P('req', ('head', 'blk'))
Inputs may be any that keep to these rules, and one draw needn't show every extreme that they name: `history_len`: one request has exactly 2048 used slots. `expert_ids`: the two experts of a token differ; within each aligned block of 64 tokens (one request, positions b * 64 onward) no expert is named by more than 16 choices, dropped ones included.
All inputs are finite; a program needn't handle non-finite values. No bound on the sum of `keep_mask` on one device may be relied on, other than what follows from the above.
Results may differ from a plain program's by a relative error of at most 0.0036.
Values may be sent and summed in bfloat16 or wider, within the bound.
No kernel may reach another device: no remote copies, remote signals or barrier semaphores. Data moves between devices by JAX's collectives and lax.ppermute only.
A program may use at most 64 MiB of HBM per device.

v0:
```python
import jax
import jax.numpy as jnp
from jax import lax
from jax.sharding import PartitionSpec as P

HD = 64
SLOT = 16
EPSILON = 1e-06


def attend_request(operands):
    (
        queries,
        keys_stretch,
        values_stretch,
        keys_cache,
        values_cache,
        keys_prefix,
        values_prefix,
        length,
    ) = operands
    heads_here = queries.shape[1] // HD
    prefix_rows = keys_prefix.shape[0]
    history_rows = keys_cache.shape[0]
    stretch_rows = queries.shape[0]
    keys_all = jnp.concatenate([keys_prefix, keys_cache, keys_stretch], 0).reshape(
        -1, heads_here, HD
    )
    values_all = jnp.concatenate([values_prefix, values_cache, values_stretch], 0).reshape(
        -1, heads_here, HD
    )
    key_pos = jnp.arange(keys_all.shape[0])
    query_pos = jnp.arange(stretch_rows)
    in_prefix = key_pos < prefix_rows
    in_history = (
        (key_pos >= prefix_rows)
        & (key_pos < prefix_rows + history_rows)
        & (key_pos - prefix_rows < length)
    )
    in_stretch = (key_pos[None, :] >= prefix_rows + history_rows) & (
        key_pos[None, :] - prefix_rows - history_rows <= query_pos[:, None]
    )
    visible = (in_prefix | in_history)[None, :] | in_stretch
    scores = jnp.einsum(
        "qhd,khd->hqk",
        queries.reshape(stretch_rows, heads_here, HD),
        keys_all,
        preferred_element_type=jnp.float32,
    ) * HD ** (-0.5)
    highest = jnp.max(jnp.where(visible[None], scores, -jnp.inf), axis=-1, keepdims=True)
    weights = jnp.where(visible[None], jnp.exp(scores - highest), 0.0)
    total = jnp.sum(weights, axis=-1, keepdims=True)
    rounded = weights.astype(jnp.bfloat16)
    mixed = jnp.einsum(
        "hqk,khd->qhd", rounded, values_all, preferred_element_type=jnp.float32
    ) / jnp.transpose(total, (1, 0, 2))
    return mixed.reshape(stretch_rows, -1).astype(jnp.bfloat16)


def extend(cache, stretch, length):
    hist = cache.shape[0]
    rows = stretch.shape[0]
    width = cache.shape[1]
    span = jnp.arange(hist + rows)
    padded_cache = jnp.concatenate([cache, jnp.zeros((rows, width), cache.dtype)], 0)
    framed = jnp.concatenate(
        [jnp.zeros((hist, width), stretch.dtype), stretch, jnp.zeros((hist, width), stretch.dtype)],
        0,
    )
    shifted = lax.dynamic_slice(framed, (hist - length, jnp.int32(0)), (hist + rows, width))
    return jnp.where((span < length)[:, None], padded_cache, shifted)


def to_positions(grown):
    groups = lax.axis_size(("head", "blk"))
    lead, rows, width = grown.shape
    parts = grown.reshape(lead, groups, rows // groups, width)
    got = lax.all_to_all(parts, ("head", "blk"), split_axis=1, concat_axis=1, tiled=True)
    return jnp.transpose(got, (0, 2, 1, 3)).reshape(lead, rows // groups, groups * width)


def body(
    x_tokens,
    query,
    key_new,
    value_new,
    cache_keys,
    cache_values,
    prefix_keys,
    prefix_values,
    history_len,
    group_ids,
    out_weight,
    norm_gain,
    router_weight,
    expert_gate,
    expert_up,
    expert_down,
    expert_ids,
    keep_mask,
):
    grown_keys = jax.vmap(extend)(cache_keys, key_new, history_len)
    grown_values = jax.vmap(extend)(cache_values, value_new, history_len)
    new_keys = to_positions(grown_keys)
    new_values = to_positions(grown_values)
    chosen_keys = jnp.take(prefix_keys, group_ids, axis=0)
    chosen_values = jnp.take(prefix_values, group_ids, axis=0)
    attended = lax.map(
        attend_request,
        (
            query,
            key_new,
            value_new,
            cache_keys,
            cache_values,
            chosen_keys,
            chosen_values,
            history_len,
        ),
    )
    requests_here = x_tokens.shape[0]
    rows_here = x_tokens.shape[1]
    width = x_tokens.shape[2]
    full_weight = lax.all_gather(out_weight, ("head", "blk"), axis=0, tiled=True)
    by_token = lax.all_to_all(attended, ("head", "blk"), split_axis=1, concat_axis=2, tiled=True)
    projected = jnp.einsum("rqf,fd->rqd", by_token, full_weight, preferred_element_type=jnp.float32)
    resid = x_tokens.astype(jnp.float32) + projected
    mean_square = jnp.mean(resid * resid, axis=-1, keepdims=True)
    normed = (resid * lax.rsqrt(mean_square + EPSILON) * norm_gain).astype(jnp.bfloat16)
    logits = jnp.dot(normed.reshape(-1, width), router_weight, preferred_element_type=jnp.float32)
    picks = expert_ids.reshape(-1, 2)
    chosen = jnp.take_along_axis(logits, picks, axis=1)
    keep = keep_mask.reshape(-1, 2)
    gate_weights = jax.nn.sigmoid(chosen - chosen[:, ::-1]) * keep.astype(jnp.float32)
    experts = router_weight.shape[1]
    slots_here = requests_here * SLOT
    block_picks = expert_ids.reshape(requests_here, rows_here * 2)
    onehot = (block_picks[:, :, None] == jnp.arange(experts)[None, None, :]).astype(jnp.int32)
    ranks = jnp.sum((jnp.cumsum(onehot, axis=1) - 1) * onehot, axis=-1)
    places = (block_picks * slots_here + jnp.arange(requests_here)[:, None] * SLOT + ranks).reshape(
        -1
    )
    sent_rows = (normed[:, :, None, :] * keep_mask[:, :, :, None].astype(jnp.bfloat16)).reshape(
        -1, width
    )
    buffer = jnp.zeros((experts * slots_here, width), jnp.bfloat16).at[places].set(sent_rows)
    holders = lax.axis_size("req") // experts
    outgoing = jnp.repeat(buffer.reshape(experts, slots_here, width), holders, axis=0)
    arrived = lax.all_to_all(outgoing, "req", split_axis=0, concat_axis=0, tiled=True)
    gathered = lax.all_gather(arrived, "head", axis=0, tiled=False)
    flat_rows = gathered.reshape(-1, width)
    gate_val = jnp.dot(flat_rows, expert_gate, preferred_element_type=jnp.float32)
    up_val = jnp.dot(flat_rows, expert_up, preferred_element_type=jnp.float32)
    hidden = (jax.nn.gelu(gate_val, approximate=True) * up_val).astype(jnp.bfloat16)
    partial = (
        jnp.dot(hidden, expert_down, preferred_element_type=jnp.float32)
        .astype(jnp.bfloat16)
        .reshape(gathered.shape)
    )
    shard_parts = lax.all_to_all(partial, "head", split_axis=0, concat_axis=0, tiled=True)
    half_sum = jnp.sum(shard_parts.astype(jnp.float32), axis=0).astype(jnp.bfloat16)
    returned = lax.all_to_all(half_sum, "req", split_axis=0, concat_axis=0, tiled=True)
    combined = jnp.sum(
        returned.reshape(experts, holders, slots_here, width), axis=1, dtype=jnp.float32
    ).reshape(experts * slots_here, width)
    picked = jnp.take(combined, places, axis=0).reshape(-1, 2, width)
    mixture = jnp.sum(picked * gate_weights[:, :, None], axis=1)
    y_out = (
        (resid.reshape(-1, width) + mixture)
        .astype(jnp.bfloat16)
        .reshape(requests_here, rows_here, width)
    )
    return (y_out, new_keys, new_values)


def solution(mesh):
    return jax.shard_map(
        body,
        mesh=mesh,
        in_specs=(
            P("req", ("head", "blk"), None),
            P("req", None, ("head", "blk")),
            P("req", None, ("head", "blk")),
            P("req", None, ("head", "blk")),
            P("req", None, ("head", "blk")),
            P("req", None, ("head", "blk")),
            P(None, None, ("head", "blk")),
            P(None, None, ("head", "blk")),
            P("req"),
            P("req"),
            P(("head", "blk"), None),
            P(),
            P(),
            P(None, ("req", "head")),
            P(None, ("req", "head")),
            P(("req", "head"), None),
            P("req", ("head", "blk"), None),
            P("req", ("head", "blk"), None),
        ),
        out_specs=(
            P("req", ("head", "blk"), None),
            P("req", ("head", "blk"), None),
            P("req", ("head", "blk"), None),
        ),
        check_vma=False,
    )
```

profile of v0, /device:TPU:2, one launch (start us, length us, event | category | flops | bytes accessed | tf_op | source)
XLA Modules:
  0.0 273.6 jit_solution(18118193608281846395)
XLA Ops:
  7.2 0.7 all-gather.4.cloned.1.call-update
  8.6 1.0 dynamic-slice_select_fusion
  9.6 0.1 copy.100
  10.4 1.2 copy.101
  11.6 1.0 copy.102
  12.6 1.0 copy.103
  13.6 0.1 copy.97
  13.8 0.2 copy.98
  14.0 0.1 copy.99
  14.2 4.3 %fusion.10 = pred[512,3072]{0,1:T(8,128)(4,1)} fusion(s32[3072]{0:T(1024)S(1)} %iota_add_fusion, pred[3072]{0:T(1024)(128)(4,1)S(1)} %get-tuple-element.73, pred[3072]{0:T(1024)(128)(4,1)S(1)} %get-tuple-element.74), kind=kLoop, calls=%fused_computation.16 | loop fusion | flops 4718592 | bytes 1591296 | tf_op jit(solution)/shard_map/while/body/eval_jaxpr/or | solution.py:43
  18.5 9.0 %fusion.72 = (f32[2,512]{1,0:T(2,128)S(1)}, bf16[2,512,3072]{1,2,0:T(8,128)(2,1)}) fusion(pred[512,3072]{0,1:T(8,128)(4,1)} %fusion.10, bf16[512,2,64]{0,2,1:T(8,128)(2,1)S(1)} %bitcast.130, bf16[512,2,64]{0,2,1:T(8,128)(2,1)S(1)} %bitcast.129, bf16[2048,2,64]{0,2,1:T(8,128)(2,1)S(1)} %bitcast.124, bf16[512,2,64]{0,2,1:T(8,128)(2,1)S(1)} %bitcast.126), kind=kOutput, calls=%fused_computation.108 | convolution fusion | flops 832048128 | bytes 8785920 | tf_op jit(solution)/shard_map/while/body/eval_jaxpr/sub | solution.py:51
  27.5 4.0 %fusion.29 = bf16[512,2,64]{0,2,1:T(8,128)(2,1)S(1)} fusion(bf16[2,512,3072]{1,2,0:T(8,128)(2,1)} %get-tuple-element.70, bf16[512,2,64]{0,2,1:T(8,128)(2,1)S(1)} %bitcast.128, bf16[2048,2,64]{0,2,1:T(8,128)(2,1)S(1)} %bitcast.123, bf16[512,2,64]{0,2,1:T(8,128)(2,1)S(1)} %bitcast.127, f32[512,2]{0,1:T(2,128)S(1)} %bitcast.133), kind=kOutput, calls=%fused_computation.39 | convolution fusion | flops 405143552 | bytes 7213056 | tf_op jit(solution)/shard_map/while/body/eval_jaxpr/hqk,khd->qhd/dot_general | solution.py:54
  31.5 0.2 copy.105
  31.7 0.5 broadcast.373
  32.2 1.4 reduce.3
  33.6 0.7 reshape.530
  34.3 4.6 %all-to-all-start = ((bf16[8,2,4096]{2,1,0:T(2,128)(2,1)}), bf16[8,2,4096]{2,1,0:T(2,128)(2,1)S(1)}, u32[]{:S(2)}, u32[]{:S(2)}) async-start(bf16[8,2,4096]{2,1,0:T(2,128)(2,1)} %reshape.530), calls=%async_computation | async-start | bytes 262144 | tf_op jit(solution)/shard_map/all_to_all | solution.py:125
  38.9 0.1 copy.107
  39.0 0.1 eq.27
  39.2 0.1 copy.110
  39.3 0.1 mul.117
  39.4 0.1 copy.111
  39.6 0.1 convert_element_type.77
  39.7 0.1 fusion.52
  39.8 0.2 reduce_window_sum.11
  40.0 0.2 select_reduce_fusion
  40.2 4.8 %all-to-all-done = bf16[8,2,4096]{2,1,0:T(2,128)(2,1)S(1)} async-done(((bf16[8,2,4096]{2,1,0:T(2,128)(2,1)}), bf16[8,2,4096]{2,1,0:T(2,128)(2,1)S(1)}, u32[]{:S(2)}, u32[]{:S(2)}) %all-to-all-start) | async-done | bytes 131104 | tf_op jit(solution)/shard_map/all_to_all | solution.py:125
  45.0 0.1 reshape.531
  45.1 0.1 copy.106
  45.3 2.2 multiply_reduce_fusion.1
  47.5 0.7 copy-done.1
  48.2 0.1 fusion.48
  48.3 0.6 copy-done.5
  48.9 0.1 mul.124
  49.1 0.1 mul.125
  49.2 1.4 scatter_custom_fusion
  50.6 0.1 broadcast_in_dim.105
  50.7 39.4 %all_to_all.40 = bf16[32,16,1024]{2,1,0:T(8,128)(2,1)} all-to-all(bf16[32,16,1024]{2,1,0:T(8,128)(2,1)S(1)} %bitcast.117), channel_id=1, replica_groups=mesh['req'=32,'head'=4,'blk'=2] {'req'}, dimensions={0} | all-to-all | bytes 2097152 | tf_op jit(solution)/shard_map/all_to_all | solution.py:149
  90.3 6.3 %fusion.42 = (bf16[1,2560,128]{2,1,0:T(8,128)(2,1)}, bf16[1,2560,128]{2,1,0:T(8,128)(2,1)}) fusion(s32[]{:T(128)} %bitcast.33, bf16[1,2048,128]{2,1,0:T(8,128)(2,1)S(1)} %broadcast.289, bf16[1,512,128]{2,1,0:T(8,128)(2,1)S(1)} %copy-done.8, bf16[1,2048,128]{2,1,0:T(8,128)(2,1)S(1)} %copy-done.4, pred[2560]{0:T(1024)(128)(4,1)S(1)} %iota_compare_fusion.4, ...), kind=kLoop, calls=%fused_computation.51 | loop fusion | flops 4587520 | bytes 3148292 | tf_op jit(solution)/shard_map/vmap(jit(_where))/select_n | solution.py:71
  96.6 3.5 %all-to-all-start.5 = ((bf16[1,8,320,128]{3,2,0,1:T(8,128)(2,1)}), bf16[1,8,320,128]{3,2,0,1:T(8,128)(2,1)S(1)}, u32[]{:S(2)}, u32[]{:S(2)}) async-start(bf16[1,8,320,128]{3,2,0,1:T(8,128)(2,1)} %bitcast.36), calls=%async_computation.5 | async-start | bytes 1310720 | tf_op jit(solution)/shard_map/all_to_all | solution.py:78
  100.2 42.8 %all-gather.6.cloned.1.call-done = bf16[128,16,1024]{2,1,0:T(8,128)(2,1)} async-done(((bf16[32,16,1024]{2,1,0:T(8,128)(2,1)}), bf16[128,16,1024]{2,1,0:T(8,128)(2,1)}) %all-gather.6.cloned.1.call-update) | async-done | bytes 4194320 | tf_op jit(solution)/shard_map/all_gather | solution.py:150
  143.0 5.6 %fusion.73 = f32[2048,352]{0,1:T(8,128)} fusion(bf16[2048,1024]{1,0:T(8,128)(2,1)} %bitcast.131, bf16[1024,352]{0,1:T(8,128)(2,1)S(1)} %copy-done.14), kind=kOutput, calls=%fused_computation.109 | convolution fusion | flops 1476395008 | bytes 7798784 | tf_op jit(solution)/shard_map/dot_general | solution.py:152
  148.6 9.2 %convolution_convert_fusion = bf16[2048,1024]{1,0:T(8,128)(2,1)} fusion(bf16[352,1024]{1,0:T(8,128)(2,1)S(1)} %copy-done, bf16[2048,1024]{1,0:T(8,128)(2,1)} %bitcast.132, bf16[1024,352]{0,1:T(8,128)(2,1)S(1)} %copy-done.15, f32[2048,352]{0,1:T(8,128)} %fusion.73), kind=kOutput, calls=%fused_computation.19 | convolution fusion | flops 2962096128 | bytes 12713984 | tf_op jit(solution)/shard_map/dot_general | solution.py:156
  157.9 54.6 %all_to_all.41 = bf16[4,32,16,1024]{3,2,1,0:T(8,128)(2,1)} all-to-all(bf16[4,32,16,1024]{3,2,1,0:T(8,128)(2,1)} %bitcast.116), channel_id=1, replica_groups=mesh['req'=32,'head'=4,'blk'=2] {'head'}, dimensions={0} | all-to-all | bytes 8388608 | tf_op jit(solution)/shard_map/all_to_all | solution.py:160
  212.4 3.5 %all-to-all-start.4 = ((bf16[1,8,320,128]{3,2,0,1:T(8,128)(2,1)}), bf16[1,8,320,128]{3,2,0,1:T(8,128)(2,1)S(1)}, u32[]{:S(2)}, u32[]{:S(2)}) async-start(bf16[1,8,320,128]{3,2,0,1:T(8,128)(2,1)} %bitcast.34), calls=%async_computation.4 | async-start | bytes 1310720 | tf_op jit(solution)/shard_map/all_to_all | solution.py:78
  216.0 4.4 %reduce_sum.69 = bf16[32,16,1024]{2,1,0:T(8,128)(2,1)} reduce(bf16[4,32,16,1024]{3,2,1,0:T(8,128)(2,1)} %all_to_all.41, bf16[]{:T(256)} %constant.108.clone.1), dimensions={0}, to_apply=%region_6.8 | reduce | flops 1572864 | bytes 5242882 | tf_op jit(solution)/shard_map/reduce_sum | solution.py:161
  220.4 7.2 %all-to-all-done.4 = bf16[1,8,320,128]{3,2,0,1:T(8,128)(2,1)S(1)} async-done(((bf16[1,8,320,128]{3,2,0,1:T(8,128)(2,1)}), bf16[1,8,320,128]{3,2,0,1:T(8,128)(2,1)S(1)}, u32[]{:S(2)}, u32[]{:S(2)}) %all-to-all-start.4) | async-done | bytes 655392 | tf_op jit(solution)/shard_map/all_to_all | solution.py:78
  227.6 8.5 %all-to-all-start.3 = ((bf16[32,16,1024]{2,1,0:T(8,128)(2,1)}), bf16[32,16,1024]{2,1,0:T(8,128)(2,1)S(1)}, u32[]{:S(2)}, u32[]{:S(2)}) async-start(bf16[32,16,1024]{2,1,0:T(8,128)(2,1)} %reduce_sum.69), calls=%async_computation.3 | async-start | bytes 2097152 | tf_op jit(solution)/shard_map/all_to_all | solution.py:162
  236.1 0.1 reduce_sum.66
  236.3 0.1 copy.112
  236.4 0.1 reshape.510
  236.6 0.1 copy.109
  236.7 0.9 copy_bitcast_fusion
  237.7 0.9 copy_bitcast_fusion.1
  238.6 0.1 fusion.74
  238.8 1.3 gather_fusion.1
  240.1 0.1 reshape.513
  240.3 0.1 copy.114
  240.4 23.4 %all-to-all-done.3 = bf16[32,16,1024]{2,1,0:T(8,128)(2,1)S(1)} async-done(((bf16[32,16,1024]{2,1,0:T(8,128)(2,1)}), bf16[32,16,1024]{2,1,0:T(8,128)(2,1)S(1)}, u32[]{:S(2)}, u32[]{:S(2)}) %all-to-all-start.3) | async-done | bytes 1048608 | tf_op jit(solution)/shard_map/all_to_all | solution.py:162
  263.9 0.2 convert_reduce_fusion
  264.1 0.8 gather_fusion
  264.9 0.3 gather.20
  265.2 0.8 multiply_reduce_fusion
  266.1 0.7 fusion.44
  (52 shorter events, 0.5 us)
Async XLA Ops:
  7.2 141.5 %copy-start = (bf16[352,1024]{1,0:T(8,128)(2,1)S(1)}, bf16[352,1024]{1,0:T(8,128)(2,1)}, u32[]{:S(2)}) copy-start(bf16[352,1024]{1,0:T(8,128)(2,1)} %param.35) | copy-start | bytes 2162692
  7.2 6.6 %copy-start.4 = (bf16[1,2048,128]{2,1,0:T(8,128)(2,1)S(1)}, bf16[1,2048,128]{2,1,0:T(8,128)(2,1)}, u32[]{:S(2)}) copy-start(bf16[1,2048,128]{2,1,0:T(8,128)(2,1)} %param.25) | copy-start | bytes 1572868
  7.2 6.8 %copy-start.8 = (bf16[1,512,128]{2,1,0:T(8,128)(2,1)S(1)}, bf16[1,512,128]{2,1,0:T(8,128)(2,1)}, u32[]{:S(2)}) copy-start(bf16[1,512,128]{2,1,0:T(8,128)(2,1)} %param.23) | copy-start | bytes 393220
  7.2 38.1 %all-gather.4.cloned.1.call-start = ((), (), s32[]{:S(2)}) async-start(), calls=%async_computation.6 | async-start | bytes 2359296 | tf_op jit(solution)/shard_map/all_gather | solution.py:124
  27.5 11.5 %copy-start.11 = (s32[1,64,2]{1,2,0:T(2,128)S(1)}, s32[1,64,2]{1,2,0:T(2,128)}, u32[]{:S(2)}) copy-start(s32[1,64,2]{1,2,0:T(2,128)} %param.36) | copy-start | bytes 1540
  27.5 11.9 %copy-start.13 = (s32[1,64,2]{1,2,0:T(2,128)S(1)}, s32[1,64,2]{1,2,0:T(2,128)}, u32[]{:S(2)}) copy-start(s32[1,64,2]{1,2,0:T(2,128)} %param.37) | copy-start | bytes 1540
  31.5 13.8 %copy-start.9 = (bf16[1,64,1024]{2,1,0:T(8,128)(2,1)S(1)}, bf16[1,64,1024]{2,1,0:T(8,128)(2,1)}, u32[]{:S(2)}) copy-start(bf16[1,64,1024]{2,1,0:T(8,128)(2,1)} %param.20) | copy-start | bytes 393220
  31.5 16.7 %copy-start.12 = (f32[1024]{0:T(1024)S(1)}, f32[1024]{0:T(1024)}, u32[]{:S(2)}) copy-start(f32[1024]{0:T(1024)} %param.31) | copy-start | bytes 12292
  34.3 10.7 %all-to-all-start = ((bf16[8,2,4096]{2,1,0:T(2,128)(2,1)}), bf16[8,2,4096]{2,1,0:T(2,128)(2,1)S(1)}, u32[]{:S(2)}, u32[]{:S(2)}) async-start(bf16[8,2,4096]{2,1,0:T(2,128)(2,1)} %reshape.530), calls=%async_computation | async-start | bytes 262144 | tf_op jit(solution)/shard_map/all_to_all | solution.py:125
  38.9 104.1 %all-gather.6.cloned.1.call-start = ((), (), s32[]{:S(2)}) async-start(), calls=%async_computation.7 | async-start | bytes 5242880 | tf_op jit(solution)/shard_map/all_gather | solution.py:150
  47.5 0.7 copy-start.1
  48.3 0.7 copy-start.5
  49.2 41.1 %copy-start.3 = (bf16[1,2048,128]{2,1,0:T(8,128)(2,1)S(1)}, bf16[1,2048,128]{2,1,0:T(8,128)(2,1)}, u32[]{:S(2)}) copy-start(bf16[1,2048,128]{2,1,0:T(8,128)(2,1)} %param.24) | copy-start | bytes 1572868
  49.2 41.1 %copy-start.7 = (bf16[1,512,128]{2,1,0:T(8,128)(2,1)S(1)}, bf16[1,512,128]{2,1,0:T(8,128)(2,1)}, u32[]{:S(2)}) copy-start(bf16[1,512,128]{2,1,0:T(8,128)(2,1)} %param.22) | copy-start | bytes 393220
  90.2 52.9 %copy-start.14 = (bf16[1024,352]{0,1:T(8,128)(2,1)S(1)}, bf16[1024,352]{0,1:T(8,128)(2,1)}, u32[]{:S(2)}) copy-start(bf16[1024,352]{0,1:T(8,128)(2,1)} %param.33) | copy-start | bytes 2162692
  96.6 61.2 %all-to-all-start.5 = ((bf16[1,8,320,128]{3,2,0,1:T(8,128)(2,1)}), bf16[1,8,320,128]{3,2,0,1:T(8,128)(2,1)S(1)}, u32[]{:S(2)}, u32[]{:S(2)}) async-start(bf16[1,8,320,128]{3,2,0,1:T(8,128)(2,1)} %bitcast.36), calls=%async_computation.5 | async-start | bytes 1310720 | tf_op jit(solution)/shard_map/all_to_all | solution.py:78
  143.0 5.6 %copy-start.15 = (bf16[1024,352]{0,1:T(8,128)(2,1)S(1)}, bf16[1024,352]{0,1:T(8,128)(2,1)}, u32[]{:S(2)}) copy-start(bf16[1024,352]{0,1:T(8,128)(2,1)} %param.34) | copy-start | bytes 2162692
  212.4 15.2 %all-to-all-start.4 = ((bf16[1,8,320,128]{3,2,0,1:T(8,128)(2,1)}), bf16[1,8,320,128]{3,2,0,1:T(8,128)(2,1)S(1)}, u32[]{:S(2)}, u32[]{:S(2)}) async-start(bf16[1,8,320,128]{3,2,0,1:T(8,128)(2,1)} %bitcast.34), calls=%async_computation.4 | async-start | bytes 1310720 | tf_op jit(solution)/shard_map/all_to_all | solution.py:78
  220.4 18.2 %copy-start.6 = (bf16[64,1024]{1,0:T(8,128)(2,1)S(1)}, bf16[64,1024]{1,0:T(8,128)(2,1)}, u32[]{:S(2)}) copy-start(bf16[64,1024]{1,0:T(8,128)(2,1)} %copy-done.5) | copy-start | bytes 393220
  220.4 18.2 %copy-start.10 = (bf16[1024,16]{0,1:T(8,128)(2,1)S(1)}, bf16[1024,16]{0,1:T(8,128)(2,1)}, u32[]{:S(2)}) copy-start(bf16[1024,16]{0,1:T(8,128)(2,1)} %param.32) | copy-start | bytes 98308
  227.6 36.2 %all-to-all-start.3 = ((bf16[32,16,1024]{2,1,0:T(8,128)(2,1)}), bf16[32,16,1024]{2,1,0:T(8,128)(2,1)S(1)}, u32[]{:S(2)}, u32[]{:S(2)}) async-start(bf16[32,16,1024]{2,1,0:T(8,128)(2,1)} %reduce_sum.69), calls=%async_computation.3 | async-start | bytes 2097152 | tf_op jit(solution)/shard_map/all_to_all | solution.py:162
  264.1 2.0 copy-start.2
Sparse Core Ops, SparseCore 0:
  9.9 30.8 all-gather.3
  90.3 52.6 all-gather.5
where the time goes:
time: 274 us
  blocking collectives  94 us (34%)
  waiting for transfers between devices  79 us (29%)
  matrix products  30.2 us (11%)
  other arithmetic  21.2 us (8%)
  starting transfers between devices  20.2 us (7%)
  between operations  15.8 us (6%)
  local copies, waits for them, and re-layouts  13.2 us (5%)
    all_to_all x1, blocking collectives, body(): lax.all_to_all(partial, 'head', split_axis=0, concat_axis=0, tiled=True)  54.6 us
    all_gather x1, waiting for transfers between devices, body(): gathered = lax.all_gather(arrived, 'head', axis=0, tiled=False)  42.8 us
    all_to_all x1, blocking collectives, body(): lax.all_to_all(outgoing, 'req', split_axis=0, concat_axis=0, tiled=True)  39.4 us
    all_to_all x1, waiting for transfers between devices, body(): lax.all_to_all(half_sum, 'req', split_axis=0, concat_axis=0, tiled=True)  23.4 us
    dot_general x1, matrix products, body(): jnp.dot(hidden, expert_down, preferred_element_type=jnp.float32)  9.24 us
    sub x1, matrix products, attend_request(): weights = jnp.where(visible[None], jnp.exp(scores - highest), 0.0)  9.01 us
    all_to_all x1, starting transfers between devices, body(): lax.all_to_all(half_sum, 'req', split_axis=0, concat_axis=0, tiled=True)  8.47 us
    all_to_all x2, waiting for transfers between devices, to_positions(): lax.all_to_all(parts, ('head', 'blk'), split_axis=1, concat_axis=1, tiled...  7.23 us
  transfers between devices with their start and end apart: 6, of which 4 were waited for; matrix products, arithmetic and copies ran while one was open for 21% of the time, Pallas kernels for 0%

commit v1 on v0

--- a/solution.py
+++ b/solution.py
@@ -75,7 +75,10 @@
     groups = lax.axis_size(("head", "blk"))
     lead, rows, width = grown.shape
     parts = grown.reshape(lead, groups, rows // groups, width)
-    got = lax.all_to_all(parts, ("head", "blk"), split_axis=1, concat_axis=1, tiled=True)
+    mat_out = lax.axis_size(("head", "blk"))
+    now = jnp.split(parts, mat_out, 1)
+    field_out = jnp.stack(now, 0)
+    got = jnp.concatenate(lax.all_to_all(field_out, ("head", "blk"), 0, 0), 1)
     return jnp.transpose(got, (0, 2, 1, 3)).reshape(lead, rows // groups, groups * width)
 
 

time: 274 us -> 279 us (1.018)
  blocking collectives: 94 us -> 39.4 us
  waiting for transfers between devices: 79 us -> 118 us
  local copies, waits for them, and re-layouts: 13.2 us -> 27.4 us
  starting transfers between devices: 20.2 us -> 26.7 us
    all_to_all x1 -> x0, blocking collectives: 54.6 us -> none  [body(): lax.all_to_all(partial, 'head', split_axis=0, concat_axis=0, tiled=True)]
    all_to_all x2 -> x3, waiting for transfers between devices: 7.23 us -> 51.1 us  [the longest x1 43.9 us: body(): lax.all_to_all(partial, 'head', split_axis=0, concat_axis=0, tiled=True)]
    unnamed x42 -> x54, local copies, waits for them, and re-layouts: 6.45 us -> 18.2 us
    all_to_all x2 -> x3, starting transfers between devices: 7.08 us -> 12.1 us  [the longest x2 7.26 us: to_positions(): got = jnp.concatenate(lax.all_to_all(field_out, ('head', 'blk'), 0, 0), 1)]
    all_gather x1, waiting for transfers between devices: 42.8 us -> 38 us  [body(): gathered = lax.all_gather(arrived, 'head', axis=0, tiled=False)]
  transfers between devices with their start and end apart: 6 -> 7, of which waited for: 4 -> 5; matrix products, arithmetic and copies ran while one was open for 21% -> 25% of each run, Pallas kernels for 0% -> 0%
where the time goes in v1:
time: 279 us; the launch traced here: 278 us
  waiting for transfers between devices  118 us (42%)
  blocking collectives  39.4 us (14%)
  matrix products  31.1 us (11%)
  local copies, waits for them, and re-layouts  27.4 us (10%)
  starting transfers between devices  26.7 us (10%)
  other arithmetic  19.1 us (7%)
  between operations  15.8 us (6%)
    all_to_all x1, waiting for transfers between devices, body(): lax.all_to_all(partial, 'head', split_axis=0, concat_axis=0, tiled=True)  43.9 us
    all_to_all x1, blocking collectives, body(): lax.all_to_all(outgoing, 'req', split_axis=0, concat_axis=0, tiled=True)  39.4 us
    all_gather x1, waiting for transfers between devices, body(): gathered = lax.all_gather(arrived, 'head', axis=0, tiled=False)  38 us
    all_to_all x1, waiting for transfers between devices, body(): lax.all_to_all(half_sum, 'req', split_axis=0, concat_axis=0, tiled=True)  23.5 us
    unnamed x54, local copies, waits for them, and re-layouts  18.2 us
    all_to_all x1, starting transfers between devices, body(): lax.all_to_all(half_sum, 'req', split_axis=0, concat_axis=0, tiled=True)  10.1 us
    sub x1, matrix products, attend_request(): weights = jnp.where(visible[None], jnp.exp(scores - highest), 0.0)  9.48 us
    dot_general x1, matrix products, body(): jnp.dot(hidden, expert_down, preferred_element_type=jnp.float32)  9.24 us
  transfers between devices with their start and end apart: 7, of which 5 were waited for; matrix products, arithmetic and copies ran while one was open for 25% of the time, Pallas kernels for 0%

profile of v1, /device:TPU:2, one launch (start us, length us, event | category | flops | bytes accessed | tf_op | source)
XLA Modules:
  0.0 277.8 jit_solution(2917030886155649860)
XLA Ops:
  7.2 0.7 all-gather.4.cloned.1.call-update
  8.6 1.0 dynamic-slice_select_fusion
  9.6 0.8 copy.112
  11.0 2.0 copy.113
  13.0 1.7 copy.114
  14.7 1.7 copy.115
  16.4 0.8 copy.109
  17.1 0.2 copy.110
  17.4 0.8 copy.111
  18.1 2.8 %fusion.10 = pred[512,3072]{0,1:T(8,128)(4,1)S(1)} fusion(s32[3072]{0:T(1024)S(1)} %iota_add_fusion, pred[3072]{0:T(1024)(128)(4,1)S(1)} %get-tuple-element.73, pred[3072]{0:T(1024)(128)(4,1)S(1)} %get-tuple-element.74), kind=kLoop, calls=%fused_computation.16 | loop fusion | flops 4718592 | bytes 1591296 | tf_op jit(solution)/shard_map/while/body/eval_jaxpr/or | solution.py:43
  20.9 9.5 %fusion.88 = (f32[2,512]{1,0:T(2,128)S(1)}, bf16[2,512,3072]{1,2,0:T(8,128)(2,1)}) fusion(pred[512,3072]{0,1:T(8,128)(4,1)S(1)} %fusion.10, bf16[512,2,64]{0,2,1:T(8,128)(2,1)} %bitcast.214, bf16[512,2,64]{0,2,1:T(8,128)(2,1)} %bitcast.213, bf16[2048,2,64]{0,2,1:T(8,128)(2,1)} %bitcast.208, bf16[512,2,64]{0,2,1:T(8,128)(2,1)} %bitcast.210), kind=kOutput, calls=%fused_computation.140 | convolution fusion | flops 832048128 | bytes 8785920 | tf_op jit(solution)/shard_map/while/body/eval_jaxpr/sub | solution.py:51
  30.4 4.3 %fusion.29 = bf16[512,2,64]{0,2,1:T(8,128)(2,1)S(1)} fusion(bf16[2,512,3072]{1,2,0:T(8,128)(2,1)} %get-tuple-element.70, bf16[512,2,64]{0,2,1:T(8,128)(2,1)} %bitcast.212, bf16[2048,2,64]{0,2,1:T(8,128)(2,1)S(1)} %bitcast.207, bf16[512,2,64]{0,2,1:T(8,128)(2,1)} %bitcast.211, f32[512,2]{0,1:T(2,128)S(1)} %bitcast.217), kind=kOutput, calls=%fused_computation.39 | convolution fusion | flops 405143552 | bytes 7213056 | tf_op jit(solution)/shard_map/while/body/eval_jaxpr/hqk,khd->qhd/dot_general | solution.py:54
  34.7 0.2 copy.117
  34.9 0.5 broadcast.373
  35.4 1.4 reduce.3
  36.8 0.7 reshape.538
  37.5 4.4 %all-to-all-start = ((bf16[8,2,4096]{2,1,0:T(2,128)(2,1)}), bf16[8,2,4096]{2,1,0:T(2,128)(2,1)S(1)}, u32[]{:S(2)}, u32[]{:S(2)}) async-start(bf16[8,2,4096]{2,1,0:T(2,128)(2,1)} %reshape.538), calls=%async_computation | async-start | bytes 262144 | tf_op jit(solution)/shard_map/all_to_all | solution.py:128
  42.6 0.1 convert_element_type.77
  42.9 0.2 reduce_window_sum.11
  43.0 0.2 select_reduce_fusion
  43.2 4.8 %all-to-all-done = bf16[8,2,4096]{2,1,0:T(2,128)(2,1)S(1)} async-done(((bf16[8,2,4096]{2,1,0:T(2,128)(2,1)}), bf16[8,2,4096]{2,1,0:T(2,128)(2,1)S(1)}, u32[]{:S(2)}, u32[]{:S(2)}) %all-to-all-start) | async-done | bytes 131104 | tf_op jit(solution)/shard_map/all_to_all | solution.py:128
  48.3 2.2 multiply_reduce_fusion.1
  50.6 0.7 copy-done.1
  51.4 0.6 copy-done.5
  52.3 1.4 scatter_custom_fusion
  53.8 39.4 %all_to_all.40 = bf16[32,16,1024]{2,1,0:T(8,128)(2,1)} all-to-all(bf16[32,16,1024]{2,1,0:T(8,128)(2,1)S(1)} %bitcast.185), channel_id=1, replica_groups=mesh['req'=32,'head'=4,'blk'=2] {'req'}, dimensions={0} | all-to-all | bytes 2097152 | tf_op jit(solution)/shard_map/all_to_all | solution.py:152
  93.4 5.8 %fusion.42 = (bf16[1,2560,128]{2,1,0:T(8,128)(2,1)S(1)}, bf16[1,2560,128]{2,1,0:T(8,128)(2,1)S(1)}) fusion(s32[]{:T(128)} %bitcast.33, bf16[1,2048,128]{2,1,0:T(8,128)(2,1)S(1)} %broadcast.289, bf16[1,512,128]{2,1,0:T(8,128)(2,1)S(1)} %copy-done.8, bf16[1,2048,128]{2,1,0:T(8,128)(2,1)S(1)} %copy-done.4, pred[2560]{0:T(1024)(128)(4,1)S(1)} %iota_compare_fusion.4, ...), kind=kLoop, calls=%fused_computation.51 | loop fusion | flops 4587520 | bytes 3148292 | tf_op jit(solution)/shard_map/vmap(jit(_where))/select_n | solution.py:71
  99.2 0.6 fusion.59
  99.8 0.6 fusion.58
  100.5 0.6 fusion.57
  101.1 0.6 fusion.56
  101.7 0.6 fusion.55
  102.4 0.6 fusion.54
  103.0 0.6 fusion.53
  103.7 0.6 fusion.52
  104.3 3.7 %all-to-all-start.5 = ((bf16[8,1,1,320,128]{4,3,2,1,0:T(8,128)(2,1)}), bf16[8,1,1,320,128]{4,3,2,1,0:T(8,128)(2,1)S(1)}, u32[]{:S(2)}, u32[]{:S(2)}) async-start(bf16[8,1,1,320,128]{4,3,2,1,0:T(8,128)(2,1)} %fusion.52), calls=%async_computation.5 | async-start | bytes 1310720 | tf_op jit(solution)/shard_map/all_to_all | solution.py:81
  108.0 38.0 %all-gather.6.cloned.1.call-done = bf16[128,16,1024]{2,1,0:T(8,128)(2,1)} async-done(((bf16[32,16,1024]{2,1,0:T(8,128)(2,1)}), bf16[128,16,1024]{2,1,0:T(8,128)(2,1)}) %all-gather.6.cloned.1.call-update) | async-done | bytes 4194320 | tf_op jit(solution)/shard_map/all_gather | solution.py:153
  146.1 5.8 %fusion.89 = f32[2048,352]{0,1:T(8,128)} fusion(bf16[2048,1024]{1,0:T(8,128)(2,1)} %bitcast.215, bf16[1024,352]{0,1:T(8,128)(2,1)} %param.33), kind=kOutput, calls=%fused_computation.141 | convolution fusion | flops 1476395008 | bytes 7798784 | tf_op jit(solution)/shard_map/dot_general | solution.py:155
  151.9 9.2 %convolution_convert_fusion = bf16[2048,1024]{1,0:T(8,128)(2,1)} fusion(bf16[352,1024]{1,0:T(8,128)(2,1)S(1)} %copy-done, bf16[2048,1024]{1,0:T(8,128)(2,1)} %bitcast.216, bf16[1024,352]{0,1:T(8,128)(2,1)S(1)} %copy-done.14, f32[2048,352]{0,1:T(8,128)} %fusion.89), kind=kOutput, calls=%fused_computation.19 | convolution fusion | flops 2962096128 | bytes 12713984 | tf_op jit(solution)/shard_map/dot_general | solution.py:159
  161.1 4.8 %all-to-all-start.2 = ((bf16[4,32,16,1024]{3,2,1,0:T(8,128)(2,1)}), bf16[4,32,16,1024]{3,2,1,0:T(8,128)(2,1)}, u32[]{:S(2)}, u32[]{:S(2)}) async-start(bf16[4,32,16,1024]{3,2,1,0:T(8,128)(2,1)} %bitcast.184), calls=%async_computation.2 | async-start | bytes 8388608 | tf_op jit(solution)/shard_map/all_to_all | solution.py:163
  165.9 0.6 fusion.67
  166.6 0.6 fusion.66
  167.2 0.6 fusion.65
  167.9 0.6 fusion.64
  168.5 0.6 fusion.63
  169.2 0.6 fusion.62
  169.8 0.6 fusion.61
  170.4 0.6 fusion.60
  171.1 43.9 %all-to-all-done.2 = bf16[4,32,16,1024]{3,2,1,0:T(8,128)(2,1)} async-done(((bf16[4,32,16,1024]{3,2,1,0:T(8,128)(2,1)}), bf16[4,32,16,1024]{3,2,1,0:T(8,128)(2,1)}, u32[]{:S(2)}, u32[]{:S(2)}) %all-to-all-start.2) | async-done | bytes 4194336 | tf_op jit(solution)/shard_map/all_to_all | solution.py:163
  214.9 3.5 %all-to-all-start.4 = ((bf16[8,1,1,320,128]{4,3,2,1,0:T(8,128)(2,1)}), bf16[8,1,1,320,128]{4,3,2,1,0:T(8,128)(2,1)S(1)}, u32[]{:S(2)}, u32[]{:S(2)}) async-start(bf16[8,1,1,320,128]{4,3,2,1,0:T(8,128)(2,1)} %fusion.60), calls=%async_computation.4 | async-start | bytes 1310720 | tf_op jit(solution)/shard_map/all_to_all | solution.py:81
  218.5 4.4 %reduce_sum.69 = bf16[32,16,1024]{2,1,0:T(8,128)(2,1)} reduce(bf16[4,32,16,1024]{3,2,1,0:T(8,128)(2,1)} %all-to-all-done.2, bf16[]{:T(256)} %constant.108.clone.1), dimensions={0}, to_apply=%region_6.8 | reduce | flops 1572864 | bytes 5242882 | tf_op jit(solution)/shard_map/reduce_sum | solution.py:164
  222.9 7.2 %all-to-all-done.4 = bf16[8,1,1,320,128]{4,3,2,1,0:T(8,128)(2,1)S(1)} async-done(((bf16[8,1,1,320,128]{4,3,2,1,0:T(8,128)(2,1)}), bf16[8,1,1,320,128]{4,3,2,1,0:T(8,128)(2,1)S(1)}, u32[]{:S(2)}, u32[]{:S(2)}) %all-to-all-start.4) | async-done | bytes 655392 | tf_op jit(solution)/shard_map/all_to_all | solution.py:81
  230.1 10.1 %all-to-all-start.3 = ((bf16[32,16,1024]{2,1,0:T(8,128)(2,1)}), bf16[32,16,1024]{2,1,0:T(8,128)(2,1)S(1)}, u32[]{:S(2)}, u32[]{:S(2)}) async-start(bf16[32,16,1024]{2,1,0:T(8,128)(2,1)} %reduce_sum.69), calls=%async_computation.3 | async-start | bytes 2097152 | tf_op jit(solution)/shard_map/all_to_all | solution.py:165
  240.5 0.1 reshape.518
  240.9 0.9 copy_bitcast_fusion
  241.8 0.9 copy_bitcast_fusion.1
  242.8 0.1 fusion.90
  242.9 1.3 gather_fusion.1
  244.6 23.5 %all-to-all-done.3 = bf16[32,16,1024]{2,1,0:T(8,128)(2,1)S(1)} async-done(((bf16[32,16,1024]{2,1,0:T(8,128)(2,1)}), bf16[32,16,1024]{2,1,0:T(8,128)(2,1)S(1)}, u32[]{:S(2)}, u32[]{:S(2)}) %all-to-all-start.3) | async-done | bytes 1048608 | tf_op jit(solution)/shard_map/all_to_all | solution.py:165
  268.0 0.2 convert_reduce_fusion
  268.3 0.8 gather_fusion
  269.1 0.3 gather.20
  269.4 0.8 multiply_reduce_fusion
  270.2 0.7 fusion.44
  (67 shorter events, 2.4 us)
Async XLA Ops:
  7.2 144.7 %copy-start = (bf16[352,1024]{1,0:T(8,128)(2,1)S(1)}, bf16[352,1024]{1,0:T(8,128)(2,1)}, u32[]{:S(2)}) copy-start(bf16[352,1024]{1,0:T(8,128)(2,1)} %param.35) | copy-start | bytes 2162692
  7.2 9.9 %copy-start.4 = (bf16[1,2048,128]{2,1,0:T(8,128)(2,1)S(1)}, bf16[1,2048,128]{2,1,0:T(8,128)(2,1)}, u32[]{:S(2)}) copy-start(bf16[1,2048,128]{2,1,0:T(8,128)(2,1)} %param.25) | copy-start | bytes 1572868
  7.2 10.2 %copy-start.8 = (bf16[1,512,128]{2,1,0:T(8,128)(2,1)S(1)}, bf16[1,512,128]{2,1,0:T(8,128)(2,1)}, u32[]{:S(2)}) copy-start(bf16[1,512,128]{2,1,0:T(8,128)(2,1)} %param.23) | copy-start | bytes 393220
  7.2 41.1 %all-gather.4.cloned.1.call-start = ((), (), s32[]{:S(2)}) async-start(), calls=%async_computation.6 | async-start | bytes 2359296 | tf_op jit(solution)/shard_map/all_gather | solution.py:127
  30.4 11.6 %copy-start.11 = (s32[1,64,2]{1,2,0:T(2,128)S(1)}, s32[1,64,2]{1,2,0:T(2,128)}, u32[]{:S(2)}) copy-start(s32[1,64,2]{1,2,0:T(2,128)} %param.36) | copy-start | bytes 1540
  30.4 12.1 %copy-start.13 = (s32[1,64,2]{1,2,0:T(2,128)S(1)}, s32[1,64,2]{1,2,0:T(2,128)}, u32[]{:S(2)}) copy-start(s32[1,64,2]{1,2,0:T(2,128)} %param.37) | copy-start | bytes 1540
  34.7 13.6 %copy-start.9 = (bf16[1,64,1024]{2,1,0:T(8,128)(2,1)S(1)}, bf16[1,64,1024]{2,1,0:T(8,128)(2,1)}, u32[]{:S(2)}) copy-start(bf16[1,64,1024]{2,1,0:T(8,128)(2,1)} %param.20) | copy-start | bytes 393220
  34.7 16.5 %copy-start.12 = (f32[1024]{0:T(1024)S(1)}, f32[1024]{0:T(1024)}, u32[]{:S(2)}) copy-start(f32[1024]{0:T(1024)} %param.31) | copy-start | bytes 12292
  37.5 10.5 %all-to-all-start = ((bf16[8,2,4096]{2,1,0:T(2,128)(2,1)}), bf16[8,2,4096]{2,1,0:T(2,128)(2,1)S(1)}, u32[]{:S(2)}, u32[]{:S(2)}) async-start(bf16[8,2,4096]{2,1,0:T(2,128)(2,1)} %reshape.538), calls=%async_computation | async-start | bytes 262144 | tf_op jit(solution)/shard_map/all_to_all | solution.py:128
  42.0 104.1 %all-gather.6.cloned.1.call-start = ((), (), s32[]{:S(2)}) async-start(), calls=%async_computation.7 | async-start | bytes 5242880 | tf_op jit(solution)/shard_map/all_gather | solution.py:153
  50.5 0.7 copy-start.1
  51.3 0.7 copy-start.5
  52.3 41.1 %copy-start.3 = (bf16[1,2048,128]{2,1,0:T(8,128)(2,1)S(1)}, bf16[1,2048,128]{2,1,0:T(8,128)(2,1)}, u32[]{:S(2)}) copy-start(bf16[1,2048,128]{2,1,0:T(8,128)(2,1)} %param.24) | copy-start | bytes 1572868
  52.3 41.1 %copy-start.7 = (bf16[1,512,128]{2,1,0:T(8,128)(2,1)S(1)}, bf16[1,512,128]{2,1,0:T(8,128)(2,1)}, u32[]{:S(2)}) copy-start(bf16[1,512,128]{2,1,0:T(8,128)(2,1)} %param.22) | copy-start | bytes 393220
  104.3 56.8 %all-to-all-start.5 = ((bf16[8,1,1,320,128]{4,3,2,1,0:T(8,128)(2,1)}), bf16[8,1,1,320,128]{4,3,2,1,0:T(8,128)(2,1)S(1)}, u32[]{:S(2)}, u32[]{:S(2)}) async-start(bf16[8,1,1,320,128]{4,3,2,1,0:T(8,128)(2,1)} %fusion.52), calls=%async_computation.5 | async-start | bytes 1310720 | tf_op jit(solution)/shard_map/all_to_all | solution.py:81
  146.1 5.8 %copy-start.14 = (bf16[1024,352]{0,1:T(8,128)(2,1)S(1)}, bf16[1024,352]{0,1:T(8,128)(2,1)}, u32[]{:S(2)}) copy-start(bf16[1024,352]{0,1:T(8,128)(2,1)} %param.34) | copy-start | bytes 2162692
  161.1 53.8 %all-to-all-start.2 = ((bf16[4,32,16,1024]{3,2,1,0:T(8,128)(2,1)}), bf16[4,32,16,1024]{3,2,1,0:T(8,128)(2,1)}, u32[]{:S(2)}, u32[]{:S(2)}) async-start(bf16[4,32,16,1024]{3,2,1,0:T(8,128)(2,1)} %bitcast.184), calls=%async_computation.2 | async-start | bytes 8388608 | tf_op jit(solution)/shard_map/all_to_all | solution.py:163
  214.9 15.2 %all-to-all-start.4 = ((bf16[8,1,1,320,128]{4,3,2,1,0:T(8,128)(2,1)}), bf16[8,1,1,320,128]{4,3,2,1,0:T(8,128)(2,1)S(1)}, u32[]{:S(2)}, u32[]{:S(2)}) async-start(bf16[8,1,1,320,128]{4,3,2,1,0:T(8,128)(2,1)} %fusion.60), calls=%async_computation.4 | async-start | bytes 1310720 | tf_op jit(solution)/shard_map/all_to_all | solution.py:81
  222.9 19.9 %copy-start.6 = (bf16[64,1024]{1,0:T(8,128)(2,1)S(1)}, bf16[64,1024]{1,0:T(8,128)(2,1)}, u32[]{:S(2)}) copy-start(bf16[64,1024]{1,0:T(8,128)(2,1)} %copy-done.5) | copy-start | bytes 393220
  222.9 19.9 %copy-start.10 = (bf16[1024,16]{0,1:T(8,128)(2,1)S(1)}, bf16[1024,16]{0,1:T(8,128)(2,1)}, u32[]{:S(2)}) copy-start(bf16[1024,16]{0,1:T(8,128)(2,1)} %param.32) | copy-start | bytes 98308
  230.1 37.9 %all-to-all-start.3 = ((bf16[32,16,1024]{2,1,0:T(8,128)(2,1)}), bf16[32,16,1024]{2,1,0:T(8,128)(2,1)S(1)}, u32[]{:S(2)}, u32[]{:S(2)}) async-start(bf16[32,16,1024]{2,1,0:T(8,128)(2,1)} %reduce_sum.69), calls=%async_computation.3 | async-start | bytes 2097152 | tf_op jit(solution)/shard_map/all_to_all | solution.py:165
  268.3 2.0 copy-start.2
Sparse Core Ops, SparseCore 0:
  9.9 30.8 all-gather.3
  93.4 52.6 all-gather.5
